TPU v7x, 256 devices: a whole 4x4x8 slice. The times are simulated.
256 devices in a mesh: cache: 8 (over y, core), dev: 32 (over x, z).
Axes of the slice: x: 4, y: 4, z: 8, core: 2. Of those that a mesh axis runs over, the one named last changes fastest.
Arguments:
- queries: bfloat16 [8, 1024, 8192], P('cache', None, 'dev'), may hold values from -8 to 8
- store_kv: bfloat16 [256, 512, 2048], P('cache', 'dev'), may hold values from -4 to 4
- self_kv: bfloat16 [8, 1024, 2048], P('cache'), may hold values from -5 to 5
- rec_states: bfloat16 [8, 512, 8192], P('cache', None, 'dev'), may hold values from -400 to 400
- norm_gain: bfloat16 [8192], P('dev'), may hold values from 0.099609375 to 1.8984375
- w_kv: bfloat16 [8192, 2048], P('dev'), may hold values from -0.0625 to 0.0625
- retrieval: int32 [8, 16], replicated, may hold values from 0 to 255, as said below
- doc_home: int32 [256], replicated, may hold values from 0 to 255, as said below
- rec_index: int32 [8, 16, 32], P('cache'), may hold values from 0 to 511, as said below
Outputs:
- attended: bfloat16 [8, 1024, 8192], P('cache', None, 'dev')
Inputs may be any that keep to these rules, and one draw needn't show every extreme that they name: `retrieval`: each request names 16 distinct documents; their store rows lie in exactly 4 of the groups of 32 consecutive rows, 4 in each. `doc_home`: every store row holds exactly one document. `rec_index`: the 32 positions of one block are distinct.
All inputs are finite; a program needn't handle non-finite values.
Results may differ from a plain program's by a relative error of at most 0.0045.
Values may be sent and summed in bfloat16 or wider, within the bound.
No kernel may reach another device: no remote copies, remote signals or barrier semaphores. Data moves between devices by JAX's collectives and lax.ppermute only.
A program may use at most 128 MiB of HBM per device.

v0:
```python
import math
import jax
import jax.numpy as jnp
from jax import lax
from jax.sharding import PartitionSpec as P

D = 8192
QH = 64
KVH = 8
HD = 128
RET = 16
CAP = 4
REC = 32
DOC_GRP = 32
eps_norm = 1e-05
tile_rows = 512


def own_head(wide_rows, head_count, head_size, chosen):
    shaped = wide_rows.reshape(wide_rows.shape[:-1] + (2, head_count, head_size))
    taken = lax.dynamic_index_in_dim(shaped, chosen, shaped.ndim - 2, keepdims=False)
    return taken.reshape(wide_rows.shape[:-1] + (2 * head_size,))


def pick_heads(wide_rows, head_count, head_size, chosen):
    shaped = wide_rows.reshape(wide_rows.shape[:-1] + (2, head_count, head_size))
    taken = jnp.take(shaped, chosen, axis=shaped.ndim - 2)
    moved = jnp.moveaxis(taken, shaped.ndim - 2, 0)
    return moved.reshape(moved.shape[:-2] + (2 * head_size,))


def shards(queries, store_kv, self_kv, rec_states, norm_gain, w_kv, retrieval, doc_home, rec_index):
    groups = lax.axis_size("cache")
    members = lax.axis_size("dev")
    my_group = lax.axis_index("cache")
    my_member = lax.axis_index("dev")
    per_device = QH // members
    ratio_heads = QH // KVH
    my_head = my_member * per_device // ratio_heads
    shard_rows = store_kv.shape[1]
    kv_width = store_kv.shape[2]
    inv_root = 1.0 / math.sqrt(HD)
    stored_at = jnp.take(doc_home, retrieval, axis=0)
    source = stored_at // DOC_GRP
    local_row = stored_at % DOC_GRP
    before = jnp.arange(RET)[None, :] < jnp.arange(RET)[:, None]
    same_home = source[:, :, None] == source[:, None, :]
    rank_within = jnp.sum((same_home & before[None, :, :]).astype(jnp.int32), axis=2)
    places = jnp.arange(CAP, dtype=jnp.int32)
    matching = (source[:, None, :] == my_group) & (rank_within[:, None, :] == places[None, :, None])
    pick_row = jnp.sum(jnp.where(matching, local_row[:, None, :], 0), axis=2)
    filled = jnp.any(matching, axis=2)
    outgoing = jnp.take(store_kv, pick_row.reshape(-1), axis=0).reshape(
        groups, CAP, shard_rows, kv_width
    )
    outgoing = jnp.where(filled[:, :, None, None], outgoing, jnp.zeros((), store_kv.dtype))
    my_source = lax.dynamic_index_in_dim(source, my_group, 0, keepdims=False)
    my_rank = lax.dynamic_index_in_dim(rank_within, my_group, 0, keepdims=False)
    slot_place = my_source * CAP + my_rank
    dest_heads = jnp.arange(members, dtype=jnp.int32) * per_device // ratio_heads
    arrived = lax.all_to_all(outgoing, "cache", split_axis=0, concat_axis=0, tiled=True)
    compact = jnp.take(arrived.reshape(groups * CAP, shard_rows, kv_width), slot_place, axis=0)
    spread = pick_heads(compact, KVH, HD, dest_heads)
    fetched = lax.all_to_all(spread, "dev", split_axis=0, concat_axis=2, tiled=True)[0]
    states = rec_states[0].astype(jnp.float32)
    partial_sq = jnp.sum(states * states, axis=1)
    total_sq = lax.psum(partial_sq, "dev")
    inv_rms = lax.rsqrt(total_sq / D + eps_norm)
    normed = (states * norm_gain.astype(jnp.float32)[None, :] * inv_rms[:, None]).astype(
        jnp.bfloat16
    )
    summed = lax.psum(jnp.dot(normed, w_kv, preferred_element_type=jnp.float32), "dev")
    redone = summed.astype(jnp.bfloat16)
    own_rows = own_head(redone.reshape(RET, REC, kv_width), KVH, HD, my_head)
    full_block = fetched.shape[1]
    positions = rec_index[0]
    onehot = positions[:, :, None] == jnp.arange(full_block, dtype=jnp.int32)[None, None, :]
    placed = jnp.einsum(
        "kib,kic->kbc", onehot.astype(jnp.bfloat16), own_rows, preferred_element_type=jnp.float32
    ).astype(jnp.bfloat16)
    replaced_at = jnp.any(onehot, axis=1)
    blocks = jnp.where(replaced_at[:, :, None], placed, fetched)
    doc_keys = blocks[:, :, :HD].reshape(-1, HD)
    doc_values = blocks[:, :, HD:].reshape(-1, HD)
    own_self = own_head(self_kv[0], KVH, HD, my_head)
    self_keys = own_self[:, :HD]
    self_values = own_self[:, HD:]
    prompt = queries.shape[1]
    head_rows = jnp.transpose(queries[0].reshape(prompt, per_device, HD), (1, 0, 2))
    block_len = min(tile_rows, prompt)
    block_count = prompt // block_len
    key_spots = jnp.arange(prompt, dtype=jnp.int32)

    def attend(pair_index):
        head_at = pair_index // block_count
        first_row = pair_index % block_count * block_len
        query_block = lax.dynamic_slice_in_dim(
            lax.dynamic_index_in_dim(head_rows, head_at, 0, keepdims=False), first_row, block_len, 0
        )
        doc_scores = (
            jnp.einsum("qd,kd->qk", query_block, doc_keys, preferred_element_type=jnp.float32)
            * inv_root
        )
        self_scores = (
            jnp.einsum("qd,kd->qk", query_block, self_keys, preferred_element_type=jnp.float32)
            * inv_root
        )
        allowed = (
            key_spots[None, :] <= (first_row + jnp.arange(block_len, dtype=jnp.int32))[:, None]
        )
        self_scores = jnp.where(allowed, self_scores, -jnp.inf)
        top = jnp.maximum(jnp.max(doc_scores, axis=1), jnp.max(self_scores, axis=1))
        doc_expd = jnp.exp(doc_scores - top[:, None])
        self_expd = jnp.exp(self_scores - top[:, None])
        total = jnp.sum(doc_expd, axis=1) + jnp.sum(self_expd, axis=1)
        weighted = jnp.dot(
            doc_expd.astype(jnp.bfloat16), doc_values, preferred_element_type=jnp.float32
        )
        weighted = weighted + jnp.dot(
            self_expd.astype(jnp.bfloat16), self_values, preferred_element_type=jnp.float32
        )
        return (weighted / total[:, None]).astype(jnp.bfloat16)

    gathered_out = lax.map(attend, jnp.arange(per_device * block_count, dtype=jnp.int32))
    result = jnp.transpose(gathered_out.reshape(per_device, prompt, HD), (1, 0, 2))
    return result.reshape(1, prompt, per_device * HD)


def solution(mesh):
    placed = (
        P("cache", None, "dev"),
        P("cache", "dev", None),
        P("cache", None, None),
        P("cache", None, "dev"),
        P("dev"),
        P("dev", None),
        P(),
        P(),
        P("cache", None, None),
    )
    return jax.shard_map(
        shards, mesh=mesh, in_specs=placed, out_specs=P("cache", None, "dev"), check_vma=False
    )
```

profile of v0, /device:TPU:8, one launch (start us, length us, event | category | flops | bytes accessed | tf_op | source)
XLA Modules:
  0.0 544.8 jit_solution(9324490959831772054)
XLA Ops:
  0.0 0.8 compare_select_fusion
  1.0 1.3 gather_fusion
  3.4 2.0 gather_fusion.1
  5.4 3.2 select_select_fusion
  8.6 5.7 %all-to-all-start = ((bf16[8,4,16,2048]{3,2,1,0:T(8,128)(2,1)}), bf16[8,4,16,2048]{3,2,1,0:T(8,128)(2,1)S(1)}, u32[]{:S(2)}, u32[]{:S(2)}) async-start(bf16[8,4,16,2048]{3,2,1,0:T(8,128)(2,1)} %select_select_fusion), calls=%async_computation | async-start | bytes 4194304 | tf_op jit(solution)/shard_map/all_to_all | solution.py:61
  14.4 25.7 %all-to-all-done = bf16[8,4,16,2048]{3,2,1,0:T(8,128)(2,1)S(1)} async-done(((bf16[8,4,16,2048]{3,2,1,0:T(8,128)(2,1)}), bf16[8,4,16,2048]{3,2,1,0:T(8,128)(2,1)S(1)}, u32[]{:S(2)}, u32[]{:S(2)}) %all-to-all-start) | async-done | bytes 2097184 | tf_op jit(solution)/shard_map/all_to_all | solution.py:61
  40.1 0.6 gather_fusion.2
  41.2 3.4 gather_fusion.3
  44.6 5.6 %copy_bitcast_fusion = bf16[32,16,16,256]{3,2,1,0:T(8,128)(2,1)} fusion(bf16[32,16,16,2,128]{4,2,3,1,0:T(8,128)(2,1)} %gather_fusion.3, pred[32]{0:T(512)(128)(4,1)S(1)} %compare_and_fusion.2), kind=kLoop, calls=%fused_computation.30 | loop fusion | flops 2097152 | bytes 8388640 | tf_op jit(solution)/shard_map/reshape | solution.py:29
  50.2 10.8 %all-to-all-start.1 = ((bf16[32,16,16,256]{3,2,1,0:T(8,128)(2,1)}), bf16[32,16,16,256]{3,2,1,0:T(8,128)(2,1)}, u32[]{:S(2)}, u32[]{:S(2)}) async-start(bf16[32,16,16,256]{3,2,1,0:T(8,128)(2,1)} %copy_bitcast_fusion), calls=%async_computation.1 | async-start | bytes 8388608 | tf_op jit(solution)/shard_map/all_to_all | solution.py:64
  61.1 155.8 %psum.14 = f32[512]{0:T(512)S(1)} all-reduce(f32[512]{0:T(512)S(1)} %fusion.25), channel_id=1, replica_groups=mesh['cache'=8,'dev'=32] {'dev'}, use_global_device_ids=true, to_apply=%region_2.3 | all-reduce | flops 512 | bytes 4096 | tf_op jit(solution)/shard_map/psum | solution.py:67
  217.0 2.7 fusion.27
  219.7 171.5 %all-reduce.1 = bf16[512,2048]{1,0:T(8,128)(2,1)S(1)} all-reduce(f32[512,2048]{1,0:T(8,128)} %fusion.27), channel_id=1, replica_groups=mesh['cache'=8,'dev'=32] {'dev'}, use_global_device_ids=true, to_apply=%region_3.4 | all-reduce | flops 1048576 | bytes 6291456 | tf_op jit(solution)/shard_map/psum | solution.py:72
  391.2 2.0 copy.40
  393.2 3.5 dynamic-slice_reduce_fusion.1
  396.8 3.6 copy.42
  400.5 3.7 dynamic-slice_reduce_fusion
  404.9 0.8 fusion.44
  405.6 2.6 copy.32
  408.2 3.0 convert_select_fusion
  411.2 2.5 fusion.43
  413.7 128.2 %while.14 = (s32[]{:T(128)}, bf16[4,512,128]{2,1,0:T(8,128)(2,1)}, s32[4]{0:T(128)S(1)}, bf16[2,1024,128]{1,2,0:T(8,128)(2,1)S(1)}, bf16[8192,128]{1,0:T(8,128)(...) while((s32[]{:T(128)}, bf16[4,512,128]{2,1,0:T(8,128)(2,1)}, ...), condition=%wide.region_12.13_spmd.clone, body=%wide.region_7.12_spmd.clone.sunk | while | flops 2453863936 | bytes 63343596 | solution.py:124
  413.7 0.7 dynamic_slice.66
  417.2 9.9 %multiply_reduce_fusion.2 = (f32[512]{0:T(512)S(1)}, f32[512,8192]{1,0:T(8,128)}) fusion(bf16[8192,128]{1,0:T(8,128)(2,1)} %get-tuple-element.316, bf16[2,1024,128]{1,2,0:T(8,128)(2,1)S(1)} %get-tuple-element.315, s32[]{:T(128)S(6)} %select_n.272, s32[]{:T(128)S(6)} %select_n.275), kind=kOutput, calls=%fused_computation.6.clone.1 | convolution fusion | flops 1082129920 | bytes 19007496 | tf_op jit(solution)/shard_map/while/body/eval_jaxpr/qd,kd->qk/dot_general | solution.py:101
  427.0 0.8 fusion.68
  428.4 8.6 %fusion.70 = f32[512]{0:T(512)S(1)} fusion(f32[512,8192]{1,0:T(8,128)} %get-tuple-element.280, f32[512]{0:T(512)S(1)} %max.13), kind=kLoop, calls=%fused_computation.7.clone.1 | loop fusion | flops 12582400 | bytes 16781312 | tf_op jit(solution)/shard_map/while/body/eval_jaxpr/reduce_sum | solution.py:115
  437.0 7.6 %fusion.69 = f32[512,128]{1,0:T(8,128)S(1)} fusion(bf16[8192,128]{1,0:T(8,128)(2,1)S(1)} %get-tuple-element.318, f32[512,8192]{1,0:T(8,128)} %get-tuple-element.280, f32[512]{0:T(512)S(1)} %max.13), kind=kOutput, calls=%fused_computation.9.clone.1 | convolution fusion | flops 1086324736 | bytes 19138560 | tf_op jit(solution)/shard_map/while/body/eval_jaxpr/dot_general | solution.py:116
  444.6 1.2 fusion.72
  445.7 0.7 dynamic_slice.66
  449.2 9.9 %multiply_reduce_fusion.2 = (f32[512]{0:T(512)S(1)}, f32[512,8192]{1,0:T(8,128)}) fusion(bf16[8192,128]{1,0:T(8,128)(2,1)} %get-tuple-element.316, bf16[2,1024,128]{1,2,0:T(8,128)(2,1)S(1)} %get-tuple-element.315, s32[]{:T(128)S(6)} %select_n.272, s32[]{:T(128)S(6)} %select_n.275), kind=kOutput, calls=%fused_computation.6.clone.1 | convolution fusion | flops 1082129920 | bytes 19007496 | tf_op jit(solution)/shard_map/while/body/eval_jaxpr/qd,kd->qk/dot_general | solution.py:101
  459.1 0.8 fusion.68
  460.4 8.6 %fusion.70 = f32[512]{0:T(512)S(1)} fusion(f32[512,8192]{1,0:T(8,128)} %get-tuple-element.280, f32[512]{0:T(512)S(1)} %max.13), kind=kLoop, calls=%fused_computation.7.clone.1 | loop fusion | flops 12582400 | bytes 16781312 | tf_op jit(solution)/shard_map/while/body/eval_jaxpr/reduce_sum | solution.py:115
  469.0 7.6 %fusion.69 = f32[512,128]{1,0:T(8,128)S(1)} fusion(bf16[8192,128]{1,0:T(8,128)(2,1)S(1)} %get-tuple-element.318, f32[512,8192]{1,0:T(8,128)} %get-tuple-element.280, f32[512]{0:T(512)S(1)} %max.13), kind=kOutput, calls=%fused_computation.9.clone.1 | convolution fusion | flops 1086324736 | bytes 19138560 | tf_op jit(solution)/shard_map/while/body/eval_jaxpr/dot_general | solution.py:116
  476.6 1.2 fusion.72
  477.8 0.7 dynamic_slice.66
  481.3 9.9 %multiply_reduce_fusion.2 = (f32[512]{0:T(512)S(1)}, f32[512,8192]{1,0:T(8,128)}) fusion(bf16[8192,128]{1,0:T(8,128)(2,1)} %get-tuple-element.316, bf16[2,1024,128]{1,2,0:T(8,128)(2,1)S(1)} %get-tuple-element.315, s32[]{:T(128)S(6)} %select_n.272, s32[]{:T(128)S(6)} %select_n.275), kind=kOutput, calls=%fused_computation.6.clone.1 | convolution fusion | flops 1082129920 | bytes 19007496 | tf_op jit(solution)/shard_map/while/body/eval_jaxpr/qd,kd->qk/dot_general | solution.py:101
  491.1 0.8 fusion.68
  492.5 8.6 %fusion.70 = f32[512]{0:T(512)S(1)} fusion(f32[512,8192]{1,0:T(8,128)} %get-tuple-element.280, f32[512]{0:T(512)S(1)} %max.13), kind=kLoop, calls=%fused_computation.7.clone.1 | loop fusion | flops 12582400 | bytes 16781312 | tf_op jit(solution)/shard_map/while/body/eval_jaxpr/reduce_sum | solution.py:115
  501.1 7.6 %fusion.69 = f32[512,128]{1,0:T(8,128)S(1)} fusion(bf16[8192,128]{1,0:T(8,128)(2,1)S(1)} %get-tuple-element.318, f32[512,8192]{1,0:T(8,128)} %get-tuple-element.280, f32[512]{0:T(512)S(1)} %max.13), kind=kOutput, calls=%fused_computation.9.clone.1 | convolution fusion | flops 1086324736 | bytes 19138560 | tf_op jit(solution)/shard_map/while/body/eval_jaxpr/dot_general | solution.py:116
  508.7 1.2 fusion.72
  509.9 0.7 dynamic_slice.66
  513.3 9.9 %multiply_reduce_fusion.2 = (f32[512]{0:T(512)S(1)}, f32[512,8192]{1,0:T(8,128)}) fusion(bf16[8192,128]{1,0:T(8,128)(2,1)} %get-tuple-element.316, bf16[2,1024,128]{1,2,0:T(8,128)(2,1)S(1)} %get-tuple-element.315, s32[]{:T(128)S(6)} %select_n.272, s32[]{:T(128)S(6)} %select_n.275), kind=kOutput, calls=%fused_computation.6.clone.1 | convolution fusion | flops 1082129920 | bytes 19007496 | tf_op jit(solution)/shard_map/while/body/eval_jaxpr/qd,kd->qk/dot_general | solution.py:101
  523.2 0.8 fusion.68
  524.5 8.6 %fusion.70 = f32[512]{0:T(512)S(1)} fusion(f32[512,8192]{1,0:T(8,128)} %get-tuple-element.280, f32[512]{0:T(512)S(1)} %max.13), kind=kLoop, calls=%fused_computation.7.clone.1 | loop fusion | flops 12582400 | bytes 16781312 | tf_op jit(solution)/shard_map/while/body/eval_jaxpr/reduce_sum | solution.py:115
  533.2 7.6 %fusion.69 = f32[512,128]{1,0:T(8,128)S(1)} fusion(bf16[8192,128]{1,0:T(8,128)(2,1)S(1)} %get-tuple-element.318, f32[512,8192]{1,0:T(8,128)} %get-tuple-element.280, f32[512]{0:T(512)S(1)} %max.13), kind=kOutput, calls=%fused_computation.9.clone.1 | convolution fusion | flops 1086324736 | bytes 19138560 | tf_op jit(solution)/shard_map/while/body/eval_jaxpr/dot_general | solution.py:116
  540.7 1.2 fusion.72
  541.9 1.7 copy.49
  543.7 1.1 reshape.294
  (75 shorter events, 4.8 us)
Async XLA Ops:
  0.0 3.4 copy-start
  0.0 0.9 copy-start.2
  1.0 1.4 copy-start.7
  8.6 31.5 %all-to-all-start = ((bf16[8,4,16,2048]{3,2,1,0:T(8,128)(2,1)}), bf16[8,4,16,2048]{3,2,1,0:T(8,128)(2,1)S(1)}, u32[]{:S(2)}, u32[]{:S(2)}) async-start(bf16[8,4,16,2048]{3,2,1,0:T(8,128)(2,1)} %select_select_fusion), calls=%async_computation | async-start | bytes 4194304 | tf_op jit(solution)/shard_map/all_to_all | solution.py:61
  50.1 10.8 %copy-start.9 = (bf16[256]{0:T(256)(128)(2,1)S(1)}, bf16[256]{0:T(256)(128)(2,1)}, u32[]{:S(2)}) copy-start(bf16[256]{0:T(256)(128)(2,1)} %param.15) | copy-start | bytes 1540
  50.1 10.8 %copy-start.3 = (bf16[1,512,256]{2,1,0:T(8,128)(2,1)S(1)}, bf16[1,512,256]{2,1,0:T(8,128)(2,1)}, u32[]{:S(2)}) copy-start(bf16[1,512,256]{2,1,0:T(8,128)(2,1)} %param.14) | copy-start | bytes 786436
  50.1 166.8 %copy-start.4 = (bf16[256,2048]{1,0:T(8,128)(2,1)S(1)}, bf16[256,2048]{1,0:T(8,128)(2,1)}, u32[]{:S(2)}) copy-start(bf16[256,2048]{1,0:T(8,128)(2,1)} %param.16) | copy-start | bytes 3145732
  50.2 355.5 %all-to-all-start.1 = ((bf16[32,16,16,256]{3,2,1,0:T(8,128)(2,1)}), bf16[32,16,16,256]{3,2,1,0:T(8,128)(2,1)}, u32[]{:S(2)}, u32[]{:S(2)}) async-start(bf16[32,16,16,256]{3,2,1,0:T(8,128)(2,1)} %copy_bitcast_fusion), calls=%async_computation.1 | async-start | bytes 8388608 | tf_op jit(solution)/shard_map/all_to_all | solution.py:64
  400.4 3.8 copy-start.5
  400.5 4.0 copy-start.8
  417.2 9.9 %copy-start.6 = (bf16[1024,128]{1,0:T(8,128)(2,1)S(1)}, bf16[1024,128]{1,0:T(8,128)(2,1)}, u32[]{:S(2)}) copy-start(bf16[1024,128]{1,0:T(8,128)(2,1)} %get-tuple-element.317) | copy-start | bytes 786436 | tf_op jit(solution)/shard_map/while
  449.2 9.9 %copy-start.6 = (bf16[1024,128]{1,0:T(8,128)(2,1)S(1)}, bf16[1024,128]{1,0:T(8,128)(2,1)}, u32[]{:S(2)}) copy-start(bf16[1024,128]{1,0:T(8,128)(2,1)} %get-tuple-element.317) | copy-start | bytes 786436 | tf_op jit(solution)/shard_map/while
  481.3 9.9 %copy-start.6 = (bf16[1024,128]{1,0:T(8,128)(2,1)S(1)}, bf16[1024,128]{1,0:T(8,128)(2,1)}, u32[]{:S(2)}) copy-start(bf16[1024,128]{1,0:T(8,128)(2,1)} %get-tuple-element.317) | copy-start | bytes 786436 | tf_op jit(solution)/shard_map/while
  513.3 9.9 %copy-start.6 = (bf16[1024,128]{1,0:T(8,128)(2,1)S(1)}, bf16[1024,128]{1,0:T(8,128)(2,1)}, u32[]{:S(2)}) copy-start(bf16[1024,128]{1,0:T(8,128)(2,1)} %get-tuple-element.317) | copy-start | bytes 786436 | tf_op jit(solution)/shard_map/while
  541.9 2.9 copy-start.1
where the time goes:
time: 546 us; the launch traced here: 545 us
  blocking collectives  327 us (60%)
  matrix products  83.4 us (15%)
  other arithmetic  47.7 us (9%)
  local copies, waits for them, and re-layouts  32.7 us (6%)
  waiting for transfers between devices  25.7 us (5%)
  starting transfers between devices  16.5 us (3%)
  loops' own time  11.3 us (2%)
    psum x1, blocking collectives, shards(): lax.psum(jnp.dot(normed, w_kv, preferred_element_type=jnp.float32), 'dev')  171 us
    psum x1, blocking collectives, shards(): total_sq = lax.psum(partial_sq, 'dev')  156 us
    dot_general x4, matrix products, attend(): jnp.einsum('qd,kd->qk', query_block, doc_keys, preferred_element_type=jnp...  39.4 us
    reduce_sum x8, other arithmetic, attend(): total = jnp.sum(doc_expd, axis=1) + jnp.sum(self_expd, axis=1)  36.5 us
    dot_general x4, matrix products, attend(): jnp.dot(doc_expd.astype(jnp.bfloat16), doc_values, preferred_element_type...  30.3 us
    all_to_all x1, waiting for transfers between devices, shards(): lax.all_to_all(outgoing, 'cache', split_axis=0, concat_axis=0, tiled=True)  25.7 us
    another operation x1, loops' own time, shards(): lax.map(attend, jnp.arange(per_device * block_count, dtype=jnp.int32))  11.3 us
  transfers between devices with their start and end apart: 2, of which 1 were waited for; matrix products, arithmetic and copies ran while one was open for 3% of the time, Pallas kernels for 0%

commit v1 on v0

--- a/solution.py
+++ b/solution.py
@@ -64,7 +64,8 @@
     fetched = lax.all_to_all(spread, "dev", split_axis=0, concat_axis=2, tiled=True)[0]
     states = rec_states[0].astype(jnp.float32)
     partial_sq = jnp.sum(states * states, axis=1)
-    total_sq = lax.psum(partial_sq, "dev")
+    terms = lax.all_gather(partial_sq, "dev", axis=0, tiled=False)
+    total_sq = terms.sum(axis=0)
     inv_rms = lax.rsqrt(total_sq / D + eps_norm)
     normed = (states * norm_gain.astype(jnp.float32)[None, :] * inv_rms[:, None]).astype(
         jnp.bfloat16

time: 546 us -> 528 us (0.967)
  blocking collectives: 327 us -> 309 us
    psum x1 -> x0, blocking collectives: 156 us -> none  [shards(): total_sq = lax.psum(partial_sq, 'dev')]
    all_gather x0 -> x1, blocking collectives: none -> 135 us  [shards(): terms = lax.all_gather(partial_sq, 'dev', axis=0, tiled=False)]
where the time goes in v1:
time: 528 us; the launch traced here: 527 us
  blocking collectives  309 us (59%)
  matrix products  83.4 us (16%)
  other arithmetic  47.8 us (9%)
  local copies, waits for them, and re-layouts  32.7 us (6%)
  waiting for transfers between devices  25.7 us (5%)
  starting transfers between devices  16.5 us (3%)
  loops' own time  11.3 us (2%)
    psum x1, blocking collectives, shards(): lax.psum(jnp.dot(normed, w_kv, preferred_element_type=jnp.float32), 'dev')  175 us
    all_gather x1, blocking collectives, shards(): terms = lax.all_gather(partial_sq, 'dev', axis=0, tiled=False)  135 us
    dot_general x4, matrix products, attend(): jnp.einsum('qd,kd->qk', query_block, doc_keys, preferred_element_type=jnp...  39.4 us
    reduce_sum x8, other arithmetic, attend(): total = jnp.sum(doc_expd, axis=1) + jnp.sum(self_expd, axis=1)  36.5 us
    dot_general x4, matrix products, attend(): jnp.dot(doc_expd.astype(jnp.bfloat16), doc_values, preferred_element_type...  30.3 us
    all_to_all x1, waiting for transfers between devices, shards(): lax.all_to_all(outgoing, 'cache', split_axis=0, concat_axis=0, tiled=True)  25.7 us
    another operation x1, loops' own time, shards(): lax.map(attend, jnp.arange(per_device * block_count, dtype=jnp.int32))  11.3 us
    all_to_all x1, starting transfers between devices, shards(): lax.all_to_all(spread, 'dev', split_axis=0, concat_axis=2, tiled=True)[0]  10.8 us
  transfers between devices with their start and end apart: 2, of which 1 were waited for; matrix products, arithmetic and copies ran while one was open for 3% of the time, Pallas kernels for 0%

profile of v1, /device:TPU:8, one launch (start us, length us, event | category | flops | bytes accessed | tf_op | source)
XLA Modules:
  0.0 526.6 jit_solution(7873913223800622854)
XLA Ops:
  0.0 0.8 compare_select_fusion
  1.0 1.3 gather_fusion
  3.4 2.0 gather_fusion.1
  5.4 3.2 select_select_fusion
  8.6 5.7 %all-to-all-start = ((bf16[8,4,16,2048]{3,2,1,0:T(8,128)(2,1)}), bf16[8,4,16,2048]{3,2,1,0:T(8,128)(2,1)S(1)}, u32[]{:S(2)}, u32[]{:S(2)}) async-start(bf16[8,4,16,2048]{3,2,1,0:T(8,128)(2,1)} %select_select_fusion), calls=%async_computation | async-start | bytes 4194304 | tf_op jit(solution)/shard_map/all_to_all | solution.py:61
  14.4 25.7 %all-to-all-done = bf16[8,4,16,2048]{3,2,1,0:T(8,128)(2,1)S(1)} async-done(((bf16[8,4,16,2048]{3,2,1,0:T(8,128)(2,1)}), bf16[8,4,16,2048]{3,2,1,0:T(8,128)(2,1)S(1)}, u32[]{:S(2)}, u32[]{:S(2)}) %all-to-all-start) | async-done | bytes 2097184 | tf_op jit(solution)/shard_map/all_to_all | solution.py:61
  40.1 0.6 gather_fusion.2
  41.2 3.4 gather_fusion.3
  44.6 5.6 %copy_bitcast_fusion = bf16[32,16,16,256]{3,2,1,0:T(8,128)(2,1)} fusion(bf16[32,16,16,2,128]{4,2,3,1,0:T(8,128)(2,1)} %gather_fusion.3, pred[32]{0:T(512)(128)(4,1)S(1)} %compare_and_fusion.2), kind=kLoop, calls=%fused_computation.30 | loop fusion | flops 2097152 | bytes 8388640 | tf_op jit(solution)/shard_map/reshape | solution.py:29
  50.2 10.8 %all-to-all-start.1 = ((bf16[32,16,16,256]{3,2,1,0:T(8,128)(2,1)}), bf16[32,16,16,256]{3,2,1,0:T(8,128)(2,1)}, u32[]{:S(2)}, u32[]{:S(2)}) async-start(bf16[32,16,16,256]{3,2,1,0:T(8,128)(2,1)} %copy_bitcast_fusion), calls=%async_computation.1 | async-start | bytes 8388608 | tf_op jit(solution)/shard_map/all_to_all | solution.py:64
  61.1 134.5 %all-gather.1 = f32[32,1,512]{2,1,0:T(1,128)S(1)} all-gather(f32[1,1,512]{2,1,0:T(1,128)S(1)} %bitcast.111), channel_id=2, replica_groups=mesh['cache'=8,'dev'=32] {'dev'}, dimensions={0}, use_global_device_ids=true | all-gather | bytes 67584 | tf_op jit(solution)/shard_map/all_gather | solution.py:67
  195.7 2.7 fusion.27
  198.5 174.5 %all-reduce.1 = bf16[512,2048]{1,0:T(8,128)(2,1)S(1)} all-reduce(f32[512,2048]{1,0:T(8,128)} %fusion.27), channel_id=1, replica_groups=mesh['cache'=8,'dev'=32] {'dev'}, use_global_device_ids=true, to_apply=%region_3.4 | all-reduce | flops 1048576 | bytes 6291456 | tf_op jit(solution)/shard_map/psum | solution.py:73
  373.0 2.0 copy.48
  375.1 3.5 dynamic-slice_reduce_fusion.1
  378.7 3.6 copy.50
  382.3 3.7 dynamic-slice_reduce_fusion
  386.7 0.8 fusion.44
  387.5 2.6 copy.40
  390.0 3.0 convert_select_fusion
  393.0 2.5 fusion.43
  395.5 128.2 %while.14 = (s32[]{:T(128)}, bf16[4,512,128]{2,1,0:T(8,128)(2,1)}, s32[4]{0:T(128)S(1)}, bf16[2,1024,128]{1,2,0:T(8,128)(2,1)S(1)}, bf16[8192,128]{1,0:T(8,128)(...) while((s32[]{:T(128)}, bf16[4,512,128]{2,1,0:T(8,128)(2,1)}, ...), condition=%wide.region_12.13_spmd.clone, body=%wide.region_7.12_spmd.clone.sunk | while | flops 2453863936 | bytes 63343596 | solution.py:125
  395.5 0.7 dynamic_slice.66
  399.0 9.9 %multiply_reduce_fusion.2 = (f32[512]{0:T(512)S(1)}, f32[512,8192]{1,0:T(8,128)}) fusion(bf16[8192,128]{1,0:T(8,128)(2,1)} %get-tuple-element.324, bf16[2,1024,128]{1,2,0:T(8,128)(2,1)S(1)} %get-tuple-element.323, s32[]{:T(128)S(6)} %select_n.272, s32[]{:T(128)S(6)} %select_n.275), kind=kOutput, calls=%fused_computation.6.clone.1 | convolution fusion | flops 1082129920 | bytes 19007496 | tf_op jit(solution)/shard_map/while/body/eval_jaxpr/qd,kd->qk/dot_general | solution.py:102
  408.9 0.8 fusion.68
  410.2 8.6 %fusion.70 = f32[512]{0:T(512)S(1)} fusion(f32[512,8192]{1,0:T(8,128)} %get-tuple-element.288, f32[512]{0:T(512)S(1)} %max.13), kind=kLoop, calls=%fused_computation.7.clone.1 | loop fusion | flops 12582400 | bytes 16781312 | tf_op jit(solution)/shard_map/while/body/eval_jaxpr/reduce_sum | solution.py:116
  418.8 7.6 %fusion.69 = f32[512,128]{1,0:T(8,128)S(1)} fusion(bf16[8192,128]{1,0:T(8,128)(2,1)S(1)} %get-tuple-element.326, f32[512,8192]{1,0:T(8,128)} %get-tuple-element.288, f32[512]{0:T(512)S(1)} %max.13), kind=kOutput, calls=%fused_computation.9.clone.1 | convolution fusion | flops 1086324736 | bytes 19138560 | tf_op jit(solution)/shard_map/while/body/eval_jaxpr/dot_general | solution.py:117
  426.4 1.2 fusion.72
  427.6 0.7 dynamic_slice.66
  431.1 9.9 %multiply_reduce_fusion.2 = (f32[512]{0:T(512)S(1)}, f32[512,8192]{1,0:T(8,128)}) fusion(bf16[8192,128]{1,0:T(8,128)(2,1)} %get-tuple-element.324, bf16[2,1024,128]{1,2,0:T(8,128)(2,1)S(1)} %get-tuple-element.323, s32[]{:T(128)S(6)} %select_n.272, s32[]{:T(128)S(6)} %select_n.275), kind=kOutput, calls=%fused_computation.6.clone.1 | convolution fusion | flops 1082129920 | bytes 19007496 | tf_op jit(solution)/shard_map/while/body/eval_jaxpr/qd,kd->qk/dot_general | solution.py:102
  440.9 0.8 fusion.68
  442.3 8.6 %fusion.70 = f32[512]{0:T(512)S(1)} fusion(f32[512,8192]{1,0:T(8,128)} %get-tuple-element.288, f32[512]{0:T(512)S(1)} %max.13), kind=kLoop, calls=%fused_computation.7.clone.1 | loop fusion | flops 12582400 | bytes 16781312 | tf_op jit(solution)/shard_map/while/body/eval_jaxpr/reduce_sum | solution.py:116
  450.9 7.6 %fusion.69 = f32[512,128]{1,0:T(8,128)S(1)} fusion(bf16[8192,128]{1,0:T(8,128)(2,1)S(1)} %get-tuple-element.326, f32[512,8192]{1,0:T(8,128)} %get-tuple-element.288, f32[512]{0:T(512)S(1)} %max.13), kind=kOutput, calls=%fused_computation.9.clone.1 | convolution fusion | flops 1086324736 | bytes 19138560 | tf_op jit(solution)/shard_map/while/body/eval_jaxpr/dot_general | solution.py:117
  458.5 1.2 fusion.72
  459.7 0.7 dynamic_slice.66
  463.1 9.9 %multiply_reduce_fusion.2 = (f32[512]{0:T(512)S(1)}, f32[512,8192]{1,0:T(8,128)}) fusion(bf16[8192,128]{1,0:T(8,128)(2,1)} %get-tuple-element.324, bf16[2,1024,128]{1,2,0:T(8,128)(2,1)S(1)} %get-tuple-element.323, s32[]{:T(128)S(6)} %select_n.272, s32[]{:T(128)S(6)} %select_n.275), kind=kOutput, calls=%fused_computation.6.clone.1 | convolution fusion | flops 1082129920 | bytes 19007496 | tf_op jit(solution)/shard_map/while/body/eval_jaxpr/qd,kd->qk/dot_general | solution.py:102
  473.0 0.8 fusion.68
  474.3 8.6 %fusion.70 = f32[512]{0:T(512)S(1)} fusion(f32[512,8192]{1,0:T(8,128)} %get-tuple-element.288, f32[512]{0:T(512)S(1)} %max.13), kind=kLoop, calls=%fused_computation.7.clone.1 | loop fusion | flops 12582400 | bytes 16781312 | tf_op jit(solution)/shard_map/while/body/eval_jaxpr/reduce_sum | solution.py:116
  483.0 7.6 %fusion.69 = f32[512,128]{1,0:T(8,128)S(1)} fusion(bf16[8192,128]{1,0:T(8,128)(2,1)S(1)} %get-tuple-element.326, f32[512,8192]{1,0:T(8,128)} %get-tuple-element.288, f32[512]{0:T(512)S(1)} %max.13), kind=kOutput, calls=%fused_computation.9.clone.1 | convolution fusion | flops 1086324736 | bytes 19138560 | tf_op jit(solution)/shard_map/while/body/eval_jaxpr/dot_general | solution.py:117
  490.5 1.2 fusion.72
  491.7 0.7 dynamic_slice.66
  495.2 9.9 %multiply_reduce_fusion.2 = (f32[512]{0:T(512)S(1)}, f32[512,8192]{1,0:T(8,128)}) fusion(bf16[8192,128]{1,0:T(8,128)(2,1)} %get-tuple-element.324, bf16[2,1024,128]{1,2,0:T(8,128)(2,1)S(1)} %get-tuple-element.323, s32[]{:T(128)S(6)} %select_n.272, s32[]{:T(128)S(6)} %select_n.275), kind=kOutput, calls=%fused_computation.6.clone.1 | convolution fusion | flops 1082129920 | bytes 19007496 | tf_op jit(solution)/shard_map/while/body/eval_jaxpr/qd,kd->qk/dot_general | solution.py:102
  505.1 0.8 fusion.68
  506.4 8.6 %fusion.70 = f32[512]{0:T(512)S(1)} fusion(f32[512,8192]{1,0:T(8,128)} %get-tuple-element.288, f32[512]{0:T(512)S(1)} %max.13), kind=kLoop, calls=%fused_computation.7.clone.1 | loop fusion | flops 12582400 | bytes 16781312 | tf_op jit(solution)/shard_map/while/body/eval_jaxpr/reduce_sum | solution.py:116
  515.0 7.6 %fusion.69 = f32[512,128]{1,0:T(8,128)S(1)} fusion(bf16[8192,128]{1,0:T(8,128)(2,1)S(1)} %get-tuple-element.326, f32[512,8192]{1,0:T(8,128)} %get-tuple-element.288, f32[512]{0:T(512)S(1)} %max.13), kind=kOutput, calls=%fused_computation.9.clone.1 | convolution fusion | flops 1086324736 | bytes 19138560 | tf_op jit(solution)/shard_map/while/body/eval_jaxpr/dot_general | solution.py:117
  522.6 1.2 fusion.72
  523.8 1.7 copy.57
  525.5 1.1 reshape.298
  (76 shorter events, 4.9 us)
Async XLA Ops:
  0.0 3.4 copy-start
  0.0 0.9 copy-start.2
  1.0 1.4 copy-start.7
  8.6 31.5 %all-to-all-start = ((bf16[8,4,16,2048]{3,2,1,0:T(8,128)(2,1)}), bf16[8,4,16,2048]{3,2,1,0:T(8,128)(2,1)S(1)}, u32[]{:S(2)}, u32[]{:S(2)}) async-start(bf16[8,4,16,2048]{3,2,1,0:T(8,128)(2,1)} %select_select_fusion), calls=%async_computation | async-start | bytes 4194304 | tf_op jit(solution)/shard_map/all_to_all | solution.py:61
  50.1 10.8 %copy-start.9 = (bf16[256]{0:T(256)(128)(2,1)S(1)}, bf16[256]{0:T(256)(128)(2,1)}, u32[]{:S(2)}) copy-start(bf16[256]{0:T(256)(128)(2,1)} %param.15) | copy-start | bytes 1540
  50.1 10.8 %copy-start.3 = (bf16[1,512,256]{2,1,0:T(8,128)(2,1)S(1)}, bf16[1,512,256]{2,1,0:T(8,128)(2,1)}, u32[]{:S(2)}) copy-start(bf16[1,512,256]{2,1,0:T(8,128)(2,1)} %param.14) | copy-start | bytes 786436
  50.1 145.6 %copy-start.4 = (bf16[256,2048]{1,0:T(8,128)(2,1)S(1)}, bf16[256,2048]{1,0:T(8,128)(2,1)}, u32[]{:S(2)}) copy-start(bf16[256,2048]{1,0:T(8,128)(2,1)} %param.16) | copy-start | bytes 3145732
  50.2 337.3 %all-to-all-start.1 = ((bf16[32,16,16,256]{3,2,1,0:T(8,128)(2,1)}), bf16[32,16,16,256]{3,2,1,0:T(8,128)(2,1)}, u32[]{:S(2)}, u32[]{:S(2)}) async-start(bf16[32,16,16,256]{3,2,1,0:T(8,128)(2,1)} %copy_bitcast_fusion), calls=%async_computation.1 | async-start | bytes 8388608 | tf_op jit(solution)/shard_map/all_to_all | solution.py:64
  382.3 3.8 copy-start.5
  382.3 4.0 copy-start.8
  399.0 9.9 %copy-start.6 = (bf16[1024,128]{1,0:T(8,128)(2,1)S(1)}, bf16[1024,128]{1,0:T(8,128)(2,1)}, u32[]{:S(2)}) copy-start(bf16[1024,128]{1,0:T(8,128)(2,1)} %get-tuple-element.325) | copy-start | bytes 786436 | tf_op jit(solution)/shard_map/while
  431.1 9.9 %copy-start.6 = (bf16[1024,128]{1,0:T(8,128)(2,1)S(1)}, bf16[1024,128]{1,0:T(8,128)(2,1)}, u32[]{:S(2)}) copy-start(bf16[1024,128]{1,0:T(8,128)(2,1)} %get-tuple-element.325) | copy-start | bytes 786436 | tf_op jit(solution)/shard_map/while
  463.1 9.9 %copy-start.6 = (bf16[1024,128]{1,0:T(8,128)(2,1)S(1)}, bf16[1024,128]{1,0:T(8,128)(2,1)}, u32[]{:S(2)}) copy-start(bf16[1024,128]{1,0:T(8,128)(2,1)} %get-tuple-element.325) | copy-start | bytes 786436 | tf_op jit(solution)/shard_map/while
  495.2 9.9 %copy-start.6 = (bf16[1024,128]{1,0:T(8,128)(2,1)S(1)}, bf16[1024,128]{1,0:T(8,128)(2,1)}, u32[]{:S(2)}) copy-start(bf16[1024,128]{1,0:T(8,128)(2,1)} %get-tuple-element.325) | copy-start | bytes 786436 | tf_op jit(solution)/shard_map/while
  523.8 2.9 copy-start.1
